TPU v7x, 256 devices: a whole 4x4x8 slice. The times are simulated.
256 devices in a mesh: dp: 2 (over core), ctx: 32 (over y, z), tensor: 4 (over x).
Axes of the slice: x: 4, y: 4, z: 8, core: 2. Of those that a mesh axis runs over, the one named last changes fastest.
Arguments:
- query_in: bfloat16 [2, 8192, 8192], P('dp', 'ctx', 'tensor'), may hold values from -6 to 6
- key_in: bfloat16 [2, 8192, 8192], P('dp', 'ctx', 'tensor'), may hold values from -6 to 6
- value_in: bfloat16 [2, 8192, 8192], P('dp', 'ctx', 'tensor'), may hold values from -6 to 6
- grad_out: bfloat16 [2, 8192, 8192], P('dp', 'ctx', 'tensor'), may hold values from -6 to 6
- seq_lengths: int32 [2, 64], P('dp'), may hold values from 1 to 512, 8192 in all within a row
- filters: bfloat16 [512, 128], P('tensor'), may hold values from -0.5 to 0.5
Outputs:
- mixed_out: bfloat16 [2, 8192, 8192], P('dp', 'ctx', 'tensor')
- grad_query: bfloat16 [2, 8192, 8192], P('dp', 'ctx', 'tensor')
- grad_key: bfloat16 [2, 8192, 8192], P('dp', 'ctx', 'tensor')
- grad_value: bfloat16 [2, 8192, 8192], P('dp', 'ctx', 'tensor')
- grad_filters: float32 [512, 128], P('tensor')
All inputs are finite; a program needn't handle non-finite values.
Results may differ from a plain program's by a relative error of at most 0.005.
Values may be sent and summed in bfloat16 or wider, within the bound.
No kernel may reach another device: no remote copies, remote signals or barrier semaphores. Data moves between devices by JAX's collectives and lax.ppermute only.
A program may use at most 192 MiB of HBM per device.

v0:
```python
import math
import jax
import jax.numpy as jnp
from jax import lax
from jax.sharding import PartitionSpec as P

GROUP = 16
FLEN = 128
GROUPS = 512


def passed_along(value, axis, steps):
    count = lax.axis_size(axis)
    initial, last = (max(0, -steps), min(count, count - steps))
    return lax.ppermute(value, axis, [(source, source + steps) for source in range(initial, last)])


def on_device(query_in, key_in, value_in, grad_out, seq_lengths, filters):
    query = query_in[0].astype(jnp.float32)
    keys = key_in[0].astype(jnp.float32)
    values = value_in[0].astype(jnp.float32)
    upstream = grad_out[0].astype(jnp.float32)
    lengths = seq_lengths[0]
    starts = jnp.cumsum(lengths) - lengths
    rows_dev, channels = query.shape
    blocks = rows_dev // FLEN
    local_groups = channels // GROUP
    offset = lax.axis_index("ctx") * rows_dev
    gated = (keys * values).astype(jnp.bfloat16)
    cotangent = (upstream * query).astype(jnp.bfloat16)
    gated_cols = gated.reshape(rows_dev, local_groups, GROUP).transpose(1, 2, 0)
    cot_cols = cotangent.reshape(rows_dev, local_groups, GROUP).transpose(1, 2, 0)
    prev_tail = passed_along(gated_cols[:, :, rows_dev - FLEN :], "ctx", 1)
    u_joined = jnp.concatenate([prev_tail, gated_cols], axis=2)
    row_ids = jnp.arange(FLEN, dtype=jnp.int32)[:, None]
    col_ids = jnp.arange(2 * FLEN, dtype=jnp.int32)[None, :]
    lag_table = row_ids - col_ids + FLEN
    inside = (lag_table >= 0) & (lag_table < FLEN)
    reversed_taps = filters[:, ::-1]
    row_pattern = jnp.concatenate(
        [
            jnp.zeros((local_groups, 1), jnp.bfloat16),
            reversed_taps,
            jnp.zeros((local_groups, FLEN), jnp.bfloat16),
        ],
        axis=1,
    )
    tiled = jnp.broadcast_to(row_pattern[:, None, :], (local_groups, FLEN, 2 * FLEN + 1))
    toeplitz = tiled.reshape(local_groups, FLEN * (2 * FLEN + 1))[:, : FLEN * 2 * FLEN].reshape(
        local_groups, FLEN, 2 * FLEN
    )

    def operator_of(block_id):
        tpos = offset + block_id * FLEN + jnp.arange(FLEN, dtype=jnp.int32)
        rpos = offset + (block_id - 1) * FLEN + jnp.arange(2 * FLEN, dtype=jnp.int32)
        doc_begin = jnp.max(jnp.where(starts[None, :] <= tpos[:, None], starts[None, :], 0), axis=1)
        inside_doc = (rpos[None, :] >= doc_begin[:, None]) & inside
        return (toeplitz * inside_doc.astype(jnp.bfloat16)[None], inside_doc.astype(jnp.float32))

    def per_block(accum, block_id):
        operator, valid = operator_of(block_id)
        window = lax.dynamic_slice_in_dim(u_joined, block_id * FLEN, 2 * FLEN, 2)
        cot_block = lax.dynamic_slice_in_dim(cot_cols, block_id * FLEN, FLEN, 2)
        mixed_rows = jnp.einsum(
            "gtr,gcr->gct", operator, window, preferred_element_type=jnp.float32
        )
        back_rows = jnp.einsum(
            "gtr,gct->gcr", operator, cot_block, preferred_element_type=jnp.float32
        )
        products = jnp.einsum("gct,gcr->gtr", cot_block, window, preferred_element_type=jnp.float32)
        accum = accum + products * valid[None]
        return (accum, (mixed_rows, back_rows))

    start_accum = jnp.zeros((local_groups, FLEN, 2 * FLEN), jnp.float32)
    accum, (mixed_blocks, back_blocks) = lax.scan(
        per_block, start_accum, jnp.arange(blocks, dtype=jnp.int32)
    )
    flat = accum.reshape(local_groups, FLEN * 2 * FLEN)
    flat = jnp.pad(flat, ((0, 0), (0, FLEN)))
    skewed = flat.reshape(local_groups, FLEN, 2 * FLEN + 1)
    lag_sums = jnp.sum(skewed, axis=1)[:, 1 : FLEN + 1]
    local_raw = lag_sums[:, ::-1]
    next_head = passed_along(cot_cols[:, :, :FLEN], "ctx", -1)
    next_operator, next_valid = operator_of(blocks)
    spill_last = jnp.einsum(
        "gtr,gct->gcr", next_operator, next_head, preferred_element_type=jnp.float32
    )[:, :, :FLEN]
    own_rows = back_blocks[:, :, :, FLEN:]
    spill_rows = jnp.concatenate([back_blocks[1:, :, :, :FLEN], spill_last[None]], axis=0)
    grad_gated = (own_rows + spill_rows).transpose(0, 3, 1, 2).reshape(rows_dev, channels)
    mixed = mixed_blocks.transpose(0, 3, 1, 2).reshape(rows_dev, channels)
    mixed_out = (query * mixed).astype(jnp.bfloat16)
    grad_query = (upstream * mixed).astype(jnp.bfloat16)
    grad_key = (grad_gated * values).astype(jnp.bfloat16)
    grad_value = (grad_gated * keys).astype(jnp.bfloat16)
    clip_limit = math.sqrt(GROUPS * FLEN)
    summed = lax.psum(local_raw, ("dp", "ctx"))
    squares = lax.psum(jnp.sum(summed * summed), "tensor")
    factor = jnp.minimum(1.0, clip_limit / jnp.sqrt(squares))
    grad_filters = summed * factor
    return (mixed_out[None], grad_query[None], grad_key[None], grad_value[None], grad_filters)


def solution(mesh):
    in_specs = (
        P("dp", "ctx", "tensor"),
        P("dp", "ctx", "tensor"),
        P("dp", "ctx", "tensor"),
        P("dp", "ctx", "tensor"),
        P("dp", None),
        P("tensor", None),
    )
    out_specs = (
        P("dp", "ctx", "tensor"),
        P("dp", "ctx", "tensor"),
        P("dp", "ctx", "tensor"),
        P("dp", "ctx", "tensor"),
        P("tensor", None),
    )
    return jax.shard_map(
        on_device, mesh=mesh, in_specs=in_specs, out_specs=out_specs, check_vma=False
    )
```

profile of v0, /device:TPU:24, one launch (start us, length us, event | category | flops | bytes accessed | tf_op | source)
XLA Modules:
  0.0 370.0 jit_solution(4789059327670511102)
XLA Ops:
  7.2 0.0 all-reduce.3.cloned.1.call-start
  7.2 1.5 copy.48
  8.7 1.9 copy.49
  10.6 0.3 fusion.34
  10.9 1.1 slice.29
  12.0 0.1 copy-done.8
  12.1 3.8 %collective-permute-start = (bf16[128,16,128]{2,1,0:T(8,128)(2,1)}, bf16[128,16,128]{2,1,0:T(8,128)(2,1)}, u32[]{:S(2)}, u32[]{:S(2)}) collective-permute-start(bf16[128,16,128]{2,1,0:T(8,128)(2,1)} %slice.29), channel_id=1, source_target_pairs={{0,4},{4,8},{8,12},{12,16},{16,20},{20,24},{24,28},{28,32},{32,36}... | collective-permute-start | bytes 1572872 | tf_op jit(solution)/shard_map/ppermute | solution.py:15
  15.9 0.5 copy.46
  16.5 2.6 copy.47
  19.1 1.5 fusion.31
  20.6 0.1 slice.31
  20.7 6.0 %collective-permute-start.1 = (bf16[128,16,128]{2,1,0:T(8,128)(2,1)S(1)}, bf16[128,16,128]{2,1,0:T(8,128)(2,1)}, u32[]{:S(2)}, u32[]{:S(2)}) collective-permute-start(bf16[128,16,128]{2,1,0:T(8,128)(2,1)S(1)} %slice.31), channel_id=1, source_target_pairs={{4,0},{8,4},{12,8},{16,12},{20,16},{24,20},{28,24},{32,28},{36,32}... | collective-permute-start | bytes 1572872 | tf_op jit(solution)/shard_map/ppermute | solution.py:15
  26.8 0.1 rev.6
  26.9 0.1 pad.9.clone
  27.0 0.1 maximum_maximum_fusion
  27.1 0.1 copy.51
  27.2 4.4 %broadcast_in_dim.81 = bf16[128,128,257]{0,2,1:T(8,128)(2,1)} broadcast(bf16[128,257]{0,1:T(8,128)(2,1)S(1)} %copy.51), dimensions={0,2} | broadcast | bytes 8487168 | tf_op jit(solution)/shard_map/broadcast_in_dim | solution.py:48
  31.7 12.9 %reshape.186 = bf16[128,32896]{0,1:T(8,128)(2,1)} reshape(bf16[128,128,257]{0,2,1:T(8,128)(2,1)} %broadcast_in_dim.81) | data formatting | bytes 16842752 | tf_op jit(solution)/shard_map/reshape | solution.py:49
  44.6 7.1 %slice.30 = bf16[128,32768]{0,1:T(8,128)(2,1)} slice(bf16[128,32896]{0,1:T(8,128)(2,1)} %reshape.186), slice={[0:128], [0:32768]} | slice | bytes 16777216 | tf_op jit(solution)/shard_map/slice | solution.py:49
  51.7 12.5 %copy.52 = bf16[128,128,256]{2,1,0:T(8,128)(2,1)} copy(bf16[128,128,256]{0,2,1:T(8,128)(2,1)} %bitcast.51) | data formatting | bytes 16777216
  64.1 0.1 copy.50
  64.2 0.1 reduce-window.4
  64.3 0.1 reduce
  64.5 0.1 select_reduce_fusion.1
  64.6 0.1 fusion.43
  64.7 1.6 pad_maximum_fusion
  66.3 37.5 %while.17 = (s32[]{:T(128)}, f32[128,128,256]{2,1,0:T(8,128)}, f32[2,128,16,128]{3,2,1,0:T(8,128)}, f32[2,128,16,256]{3,2,1,0:T(8,128)}, s32[2]{0:T(128)S(1)}, /...) while((s32[]{:T(128)}, f32[128,128,256]{2,1,0:T(8,128)}, ...), condition=%wide.region_3.4_spmd.clone, body=%wide.region_1.3_spmd.clone.sunk | while | flops 423944448 | bytes 90641992 | solution.py:75
  66.3 0.6 dynamic_slice.39
  67.5 0.1 select_reduce_fusion.3
  68.3 0.1 fusion.60
  68.4 7.9 %select_add_fusion.2 = f32[128,128,256]{2,1,0:T(8,128)} fusion(f32[128,128,256]{2,1,0:T(8,128)} %get-tuple-element.335, f32[128,256]{1,0:T(8,128)S(1)} %get-tuple-element.316, pred[]{:T(512)S(6)} %compare.4, bf16[128,16,384]{2,1,0:T(8,128)(2,1)S(1)} %get-tuple-element.356, s32[]{:T(128)S(6)} %select_n.32, ...), kind=kOutput, calls=%fused_computation.1.clone.1 | convolution fusion | flops 146800640 | bytes 35258376 | tf_op jit(solution)/shard_map/while/body/eval_jaxpr/gct,gcr->gtr/dot_general | solution.py:70
  76.3 2.7 bitcast_dynamic-update-slice_fusion.2
  79.0 3.3 fusion.61
  82.3 0.6 dynamic_slice.39
  83.5 0.1 select_reduce_fusion.3
  84.3 0.1 fusion.60
  84.4 12.9 %select_add_fusion.2 = f32[128,128,256]{2,1,0:T(8,128)} fusion(f32[128,128,256]{2,1,0:T(8,128)} %get-tuple-element.335, f32[128,256]{1,0:T(8,128)S(1)} %get-tuple-element.316, pred[]{:T(512)S(6)} %compare.4, bf16[128,16,384]{2,1,0:T(8,128)(2,1)S(1)} %get-tuple-element.356, s32[]{:T(128)S(6)} %select_n.32, ...), kind=kOutput, calls=%fused_computation.1.clone.1 | convolution fusion | flops 146800640 | bytes 35258376 | tf_op jit(solution)/shard_map/while/body/eval_jaxpr/gct,gcr->gtr/dot_general | solution.py:70
  97.3 0.5 copy-done
  97.9 2.6 bitcast_dynamic-update-slice_fusion.2
  100.5 3.3 fusion.61
  103.8 1.3 slice.24
  105.1 3.6 fusion.38
  108.6 1.9 fusion.37
  110.6 2.9 copy.55
  113.5 4.1 %reshape.190 = f32[1,256,2048]{1,2,0:T(8,128)} reshape(f32[2,128,128,16]{1,0,3,2:T(2,128)} %copy.55) | data formatting | bytes 4194304 | tf_op jit(solution)/shard_map/reshape | solution.py:90
  117.6 2.9 fusion.33
  120.5 17.8 %copy.62 = f32[128,128,256]{0,2,1:T(8,128)} copy(f32[128,128,256]{2,1,0:T(8,128)} %get-tuple-element.146) | data formatting | bytes 33554432 | tf_op jit(solution)/shard_map/reshape | solution.py:78
  138.4 13.3 %pad.4 = f32[128,32896]{0,1:T(8,128)} pad(f32[128,32768]{0,1:T(8,128)} %bitcast.48, f32[]{:T(128)} %constant.68.clone.1), padding=0_0x0_128 | pad | bytes 33619972 | tf_op jit(solution)/shard_map/jit(_pad)/pad | solution.py:79
  151.7 17.5 %reshape.192 = f32[128,128,257]{0,2,1:T(8,128)} reshape(f32[128,32896]{0,1:T(8,128)} %pad.4) | data formatting | bytes 33685504 | tf_op jit(solution)/shard_map/reshape | solution.py:80
  169.2 6.7 %reduce_sum.18 = f32[128,257]{0,1:T(8,128)S(1)} reduce(f32[128,128,257]{0,2,1:T(8,128)} %reshape.192, f32[]{:T(128)} %constant.68.clone.1), dimensions={1}, to_apply=%region_5.6 | reduce | flops 4177792 | bytes 16974340 | tf_op jit(solution)/shard_map/reduce_sum | solution.py:81
  175.9 0.6 rev.7
  176.5 0.0 all-reduce.3.cloned.1.call-update
  176.6 4.6 %copy.53 = f32[2,128,128,16]{1,0,3,2:T(2,128)} copy(f32[2,128,128,16]{1,3,2,0:T(8,128)} %bitcast.7) | data formatting | bytes 4194304 | tf_op jit(solution)/shard_map/transpose | solution.py:91
  181.1 4.0 %reshape.188 = f32[1,256,2048]{1,2,0:T(8,128)} reshape(f32[2,128,128,16]{1,0,3,2:T(2,128)} %copy.53) | data formatting | bytes 4194304 | tf_op jit(solution)/shard_map/reshape | solution.py:91
  185.2 3.3 fusion.32
  188.5 2.4 copy.59
  190.9 1.4 copy.60
  192.3 1.4 copy.57
  193.7 153.2 %all-reduce.3.cloned.1.call-done = f32[128,128]{0,1:T(8,128)} async-done(((f32[128,128]{0,1:T(8,128)}), f32[128,128]{0,1:T(8,128)}) %all-reduce.3.cloned.1.call-update) | async-done | bytes 65552 | tf_op jit(solution)/shard_map/psum | solution.py:97
  347.0 1.5 multiply_reduce_fusion
  348.4 1.4 copy.58
  349.8 11.0 %psum.15 = f32[]{:T(128)} all-reduce(f32[]{:T(128)} %multiply_reduce_fusion), channel_id=1, replica_groups=mesh['dp'=2,'ctx'=32,'tensor'=4] {'tensor'}, use_global_device_ids=true, to_apply=%region_8.9 | all-reduce | flops 1 | bytes 8 | tf_op jit(solution)/shard_map/psum | solution.py:98
  361.6 0.8 broadcast_multiply_fusion
  362.4 0.7 copy.61
  (46 shorter events, 0.1 us)
Async XLA Ops:
  7.2 339.8 %all-reduce.3.cloned.1.call-start = ((), (), s32[]{:S(2)}) async-start(), calls=%async_computation | async-start | bytes 131072 | tf_op jit(solution)/shard_map/psum | solution.py:97
  8.7 3.3 copy-start.4
  8.7 7.2 %copy-start.11 = (bf16[1,256,2048]{2,1,0:T(8,128)(2,1)S(1)}, bf16[1,256,2048]{2,1,0:T(8,128)(2,1)}, u32[]{:S(2)}) copy-start(bf16[1,256,2048]{2,1,0:T(8,128)(2,1)} %param.8) | copy-start | bytes 3145732
  10.6 5.9 %copy-start.6 = (bf16[1,256,2048]{1,2,0:T(8,128)(2,1)}, bf16[1,256,2048]{1,2,0:T(8,128)(2,1)S(1)}, u32[]{:S(2)}) copy-start(bf16[1,256,2048]{1,2,0:T(8,128)(2,1)S(1)} %copy.49) | copy-start | bytes 3145732
  10.9 1.2 copy-start.8
  12.1 52.6 %collective-permute-start = (bf16[128,16,128]{2,1,0:T(8,128)(2,1)}, bf16[128,16,128]{2,1,0:T(8,128)(2,1)}, u32[]{:S(2)}, u32[]{:S(2)}) collective-permute-start(bf16[128,16,128]{2,1,0:T(8,128)(2,1)} %slice.29), channel_id=1, source_target_pairs={{0,4},{4,8},{8,12},{12,16},{16,20},{20,24},{24,28},{28,32},{32,36}... | collective-permute-start | bytes 1572872 | tf_op jit(solution)/shard_map/ppermute | solution.py:15
  16.5 4.3 %copy-start.1 = (bf16[1,256,2048]{1,2,0:T(8,128)(2,1)}, bf16[1,256,2048]{1,2,0:T(8,128)(2,1)S(1)}, u32[]{:S(2)}) copy-start(bf16[1,256,2048]{1,2,0:T(8,128)(2,1)S(1)} %copy.46) | copy-start | bytes 3145732
  16.5 10.3 %copy-start.12 = (bf16[128,128]{1,0:T(8,128)(2,1)S(1)}, bf16[128,128]{1,0:T(8,128)(2,1)}, u32[]{:S(2)}) copy-start(bf16[128,128]{1,0:T(8,128)(2,1)} %param.13) | copy-start | bytes 98308
  20.7 84.3 %collective-permute-start.1 = (bf16[128,16,128]{2,1,0:T(8,128)(2,1)S(1)}, bf16[128,16,128]{2,1,0:T(8,128)(2,1)}, u32[]{:S(2)}, u32[]{:S(2)}) collective-permute-start(bf16[128,16,128]{2,1,0:T(8,128)(2,1)S(1)} %slice.31), channel_id=1, source_target_pairs={{4,0},{8,4},{12,8},{16,12},{20,16},{24,20},{28,24},{32,28},{36,32}... | collective-permute-start | bytes 1572872 | tf_op jit(solution)/shard_map/ppermute | solution.py:15
  51.7 12.5 %copy-start.13 = (s32[1,64]{1,0:T(1,128)S(1)}, s32[1,64]{1,0:T(1,128)}, u32[]{:S(2)}) copy-start(s32[1,64]{1,0:T(1,128)} %param.12) | copy-start | bytes 772
  68.4 7.9 %copy-start = (bf16[128,128,256]{2,1,0:T(8,128)(2,1)S(1)}, bf16[128,128,256]{2,1,0:T(8,128)(2,1)}, u32[]{:S(2)}) copy-start(bf16[128,128,256]{2,1,0:T(8,128)(2,1)} %get-tuple-element.359) | copy-start | bytes 25165828 | tf_op jit(solution)/shard_map/while
  84.4 13.5 %copy-start = (bf16[128,128,256]{2,1,0:T(8,128)(2,1)S(1)}, bf16[128,128,256]{2,1,0:T(8,128)(2,1)}, u32[]{:S(2)}) copy-start(bf16[128,128,256]{2,1,0:T(8,128)(2,1)} %get-tuple-element.359) | copy-start | bytes 25165828 | tf_op jit(solution)/shard_map/while
  113.5 4.1 %copy-start.5 = (bf16[1,256,2048]{1,2,0:T(8,128)(2,1)S(1)}, bf16[1,256,2048]{1,2,0:T(8,128)(2,1)}, u32[]{:S(2)}) copy-start(bf16[1,256,2048]{1,2,0:T(8,128)(2,1)} %copy-done.4) | copy-start | bytes 3145732
  113.5 4.1 %copy-start.7 = (bf16[1,256,2048]{1,2,0:T(8,128)(2,1)S(1)}, bf16[1,256,2048]{1,2,0:T(8,128)(2,1)}, u32[]{:S(2)}) copy-start(bf16[1,256,2048]{1,2,0:T(8,128)(2,1)} %copy-done.6) | copy-start | bytes 3145732
  181.1 4.1 %copy-start.2 = (bf16[1,256,2048]{1,2,0:T(8,128)(2,1)S(1)}, bf16[1,256,2048]{1,2,0:T(8,128)(2,1)}, u32[]{:S(2)}) copy-start(bf16[1,256,2048]{1,2,0:T(8,128)(2,1)} %copy-done.1) | copy-start | bytes 3145732
  181.1 4.1 %copy-start.3 = (bf16[1,256,2048]{1,2,0:T(8,128)(2,1)S(1)}, bf16[1,256,2048]{1,2,0:T(8,128)(2,1)}, u32[]{:S(2)}) copy-start(bf16[1,256,2048]{1,2,0:T(8,128)(2,1)} %copy.47) | copy-start | bytes 3145732
  188.5 3.8 %copy-start.10 = (bf16[1,256,2048]{1,2,0:T(8,128)(2,1)S(1)}, bf16[1,256,2048]{1,2,0:T(8,128)(2,1)}, u32[]{:S(2)}) copy-start(bf16[1,256,2048]{1,2,0:T(8,128)(2,1)} %get-tuple-element.252) | copy-start | bytes 3145732
  188.5 160.0 %copy-start.9 = (bf16[1,256,2048]{1,2,0:T(8,128)(2,1)S(1)}, bf16[1,256,2048]{1,2,0:T(8,128)(2,1)}, u32[]{:S(2)}) copy-start(bf16[1,256,2048]{1,2,0:T(8,128)(2,1)} %get-tuple-element.251) | copy-start | bytes 3145732
Sparse Core Ops, SparseCore 0:
  176.7 170.2 all-reduce.2
where the time goes:
time: 372 us; the launch traced here: 370 us
  waiting for transfers between devices  153 us (41%)
  local copies, waits for them, and re-layouts  120 us (32%)
  matrix products  36.2 us (10%)
  other arithmetic  21.4 us (6%)
  between operations  15 us (4%)
  blocking collectives  11 us (3%)
  starting transfers between devices  9.89 us (3%)
    psum x1, waiting for transfers between devices, on_device(): summed = lax.psum(local_raw, ('dp', 'ctx'))  153 us
    unnamed x36, local copies, waits for them, and re-layouts  26.6 us
    dot_general x2, matrix products, per_block(): jnp.einsum('gct,gcr->gtr', cot_block, window, preferred_element_type=jnp....  20.8 us
    reshape x1, local copies, waits for them, and re-layouts, on_device(): flat = accum.reshape(local_groups, FLEN * 2 * FLEN)  17.8 us
    reshape x1, local copies, waits for them, and re-layouts, on_device(): skewed = flat.reshape(local_groups, FLEN, 2 * FLEN + 1)  17.5 us
    pad x1, local copies, waits for them, and re-layouts, on_device(): flat = jnp.pad(flat, ((0, 0), (0, FLEN)))  13.3 us
    reshape x1, local copies, waits for them, and re-layouts, on_device(): tiled.reshape(local_groups, FLEN * (2 * FLEN + 1))[:, :FLEN * 2 * FLEN]  12.9 us
    psum x1, blocking collectives, on_device(): squares = lax.psum(jnp.sum(summed * summed), 'tensor')  11 us
  transfers between devices with their start and end apart: 3, of which 1 were waited for; matrix products, arithmetic and copies ran while one was open for 26% of the time, Pallas kernels for 0%

commit v1 on v0

--- a/solution.py
+++ b/solution.py
@@ -94,7 +94,7 @@
     grad_key = (grad_gated * values).astype(jnp.bfloat16)
     grad_value = (grad_gated * keys).astype(jnp.bfloat16)
     clip_limit = math.sqrt(GROUPS * FLEN)
-    summed = lax.psum(local_raw, ("dp", "ctx"))
+    summed = jnp.sum(lax.all_gather(local_raw, ("dp", "ctx")), axis=0)
     squares = lax.psum(jnp.sum(summed * summed), "tensor")
     factor = jnp.minimum(1.0, clip_limit / jnp.sqrt(squares))
     grad_filters = summed * factor

time: 372 us -> 260 us (0.70)
  waiting for transfers between devices: 153 us -> 38.3 us
  local copies, waits for them, and re-layouts: 120 us -> 124 us
    psum x1 -> x0, waiting for transfers between devices: 153 us -> none  [on_device(): summed = lax.psum(local_raw, ('dp', 'ctx'))]
    all_gather x0 -> x1, waiting for transfers between devices: none -> 28.5 us  [on_device(): summed = jnp.sum(lax.all_gather(local_raw, ('dp', 'ctx')), axis=0)]
    ppermute x2, waiting for transfers between devices: 0.01 us -> 9.79 us  [passed_along(): lax.ppermute(value, axis, [(source, source + steps) for source in range(i...]
    unnamed x36 -> x33, local copies, waits for them, and re-layouts: 26.6 us -> 30.8 us
  transfers between devices with their start and end apart: 3 -> 3, of which waited for: 1 -> 2; matrix products, arithmetic and copies ran while one was open for 26% -> 30% of each run, Pallas kernels for 0% -> 0%
where the time goes in v1:
time: 260 us; the launch traced here: 258 us
  local copies, waits for them, and re-layouts  124 us (48%)
  waiting for transfers between devices  38.3 us (15%)
  matrix products  36.1 us (14%)
  other arithmetic  20 us (8%)
  between operations  15 us (6%)
  blocking collectives  11 us (4%)
  starting transfers between devices  10.1 us (4%)
  loops' own time  2.72 us (1%)
    unnamed x33, local copies, waits for them, and re-layouts  30.8 us
    all_gather x1, waiting for transfers between devices, on_device(): summed = jnp.sum(lax.all_gather(local_raw, ('dp', 'ctx')), axis=0)  28.5 us
    dot_general x2, matrix products, per_block(): jnp.einsum('gct,gcr->gtr', cot_block, window, preferred_element_type=jnp....  20.8 us
    reshape x1, local copies, waits for them, and re-layouts, on_device(): flat = accum.reshape(local_groups, FLEN * 2 * FLEN)  17.8 us
    reshape x1, local copies, waits for them, and re-layouts, on_device(): skewed = flat.reshape(local_groups, FLEN, 2 * FLEN + 1)  17.5 us
    pad x1, local copies, waits for them, and re-layouts, on_device(): flat = jnp.pad(flat, ((0, 0), (0, FLEN)))  13.3 us
    reshape x1, local copies, waits for them, and re-layouts, on_device(): tiled.reshape(local_groups, FLEN * (2 * FLEN + 1))[:, :FLEN * 2 * FLEN]  12.9 us
    psum x1, blocking collectives, on_device(): squares = lax.psum(jnp.sum(summed * summed), 'tensor')  11 us
  transfers between devices with their start and end apart: 3, of which 2 were waited for; matrix products, arithmetic and copies ran while one was open for 30% of the time, Pallas kernels for 0%

profile of v1, /device:TPU:24, one launch (start us, length us, event | category | flops | bytes accessed | tf_op | source)
XLA Modules:
  0.0 257.6 jit_solution(7773544835328440357)
XLA Ops:
  7.2 1.6 copy.63
  8.8 1.9 copy.64
  10.7 0.3 fusion.34
  11.0 1.0 copy-done.8
  12.0 0.9 slice.29
  12.9 3.8 %collective-permute-start = (bf16[128,16,128]{2,1,0:T(8,128)(2,1)}, bf16[128,16,128]{2,1,0:T(8,128)(2,1)}, u32[]{:S(2)}, u32[]{:S(2)}) collective-permute-start(bf16[128,16,128]{2,1,0:T(8,128)(2,1)} %slice.29), channel_id=1, source_target_pairs={{0,4},{4,8},{8,12},{12,16},{16,20},{20,24},{24,28},{28,32},{32,36}... | collective-permute-start | bytes 1572872 | tf_op jit(solution)/shard_map/ppermute | solution.py:15
  16.7 0.5 copy.61
  17.3 2.6 %copy.62 = bf16[1,256,2048]{1,2,0:T(8,128)(2,1)} copy(bf16[1,256,2048]{2,1,0:T(8,128)(2,1)} %param.11) | data formatting | bytes 2097152 | tf_op args[3]
  19.9 0.1 rev.6
  20.0 0.1 pad.9.clone
  20.1 0.1 maximum_maximum_fusion
  20.2 0.1 copy.66
  20.3 4.4 %broadcast_in_dim.81 = bf16[128,128,257]{0,2,1:T(8,128)(2,1)} broadcast(bf16[128,257]{0,1:T(8,128)(2,1)S(1)} %copy.66), dimensions={0,2} | broadcast | bytes 8487168 | tf_op jit(solution)/shard_map/broadcast_in_dim | solution.py:48
  24.7 12.9 %reshape.186 = bf16[128,32896]{0,1:T(8,128)(2,1)} reshape(bf16[128,128,257]{0,2,1:T(8,128)(2,1)} %broadcast_in_dim.81) | data formatting | bytes 16842752 | tf_op jit(solution)/shard_map/reshape | solution.py:49
  37.7 7.1 %slice.30 = bf16[128,32768]{0,1:T(8,128)(2,1)} slice(bf16[128,32896]{0,1:T(8,128)(2,1)} %reshape.186), slice={[0:128], [0:32768]} | slice | bytes 16777216 | tf_op jit(solution)/shard_map/slice | solution.py:49
  44.8 12.2 %copy.67 = bf16[128,128,256]{2,1,0:T(8,128)(2,1)} copy(bf16[128,128,256]{0,2,1:T(8,128)(2,1)} %bitcast.55) | data formatting | bytes 16777216
  56.9 0.1 copy.65
  57.0 0.1 reduce-window.4
  57.1 0.1 reduce
  57.3 1.5 fusion.31
  58.8 1.6 pad_maximum_fusion
  60.3 37.5 %while.17 = (s32[]{:T(128)}, f32[128,128,256]{2,1,0:T(8,128)}, f32[2,128,16,128]{3,2,1,0:T(8,128)}, f32[2,128,16,256]{3,2,1,0:T(8,128)}, s32[2]{0:T(128)S(1)}, /...) while((s32[]{:T(128)}, f32[128,128,256]{2,1,0:T(8,128)}, ...), condition=%wide.region_3.4_spmd.clone, body=%wide.region_1.3_spmd.clone.sunk | while | flops 423944448 | bytes 90641992 | solution.py:75
  60.4 0.6 dynamic_slice.39
  61.6 0.1 select_reduce_fusion.3
  62.4 0.1 fusion.60
  62.5 7.9 %select_add_fusion.2 = f32[128,128,256]{2,1,0:T(8,128)} fusion(f32[128,128,256]{2,1,0:T(8,128)} %get-tuple-element.350, f32[128,256]{1,0:T(8,128)S(1)} %get-tuple-element.331, pred[]{:T(512)S(6)} %compare.4, bf16[128,16,384]{2,1,0:T(8,128)(2,1)S(1)} %get-tuple-element.371, s32[]{:T(128)S(6)} %select_n.32, ...), kind=kOutput, calls=%fused_computation.1.clone.1 | convolution fusion | flops 146800640 | bytes 35258376 | tf_op jit(solution)/shard_map/while/body/eval_jaxpr/gct,gcr->gtr/dot_general | solution.py:70
  70.4 2.7 %bitcast_dynamic-update-slice_fusion.2 = f32[2,128,16,256]{3,2,1,0:T(8,128)} fusion(f32[2,128,16,256]{3,2,1,0:T(8,128)} %get-tuple-element.352, s32[]{:T(128)} %get-tuple-element.349, bf16[128,128,256]{2,1,0:T(8,128)(2,1)S(1)} %copy-done, bf16[128,256]{1,0:T(8,128)(2,1)S(1)} %get-tuple-element.332, bf16[128,16,256]{2,1,0:T(8,128)(2,1)S(1)} %get-tuple-element.370, ...), kind=kOutput, calls=%fused_computation.8.clone.1 | convolution fusion | flops 138412032 | bytes 11076100 | tf_op jit(solution)/shard_map/while/body/eval_jaxpr/gtr,gct->gcr/dot_general | solution.py:67
  73.0 3.3 %fusion.61 = f32[2,128,16,128]{3,2,1,0:T(8,128)} fusion(f32[2,128,16,128]{3,2,1,0:T(8,128)} %get-tuple-element.351, s32[]{:T(128)} %get-tuple-element.349, bf16[128,128,256]{2,1,0:T(8,128)(2,1)S(1)} %copy-done, bf16[128,256]{1,0:T(8,128)(2,1)S(1)} %get-tuple-element.332, bf16[128,16,384]{2,1,0:T(8,128)(2,1)S(1)} %get-tuple-element.371, s32[]{:T(128)S(6)} %select_n.32), kind=kOutput, calls=%fused_computation.10.clone.1 | convolution fusion | flops 138412032 | bytes 10551812 | tf_op jit(solution)/shard_map/while/body/eval_jaxpr/gtr,gcr->gct/dot_general | solution.py:64
  76.3 0.6 dynamic_slice.39
  77.6 0.1 select_reduce_fusion.3
  78.4 0.1 fusion.60
  78.5 12.9 %select_add_fusion.2 = f32[128,128,256]{2,1,0:T(8,128)} fusion(f32[128,128,256]{2,1,0:T(8,128)} %get-tuple-element.350, f32[128,256]{1,0:T(8,128)S(1)} %get-tuple-element.331, pred[]{:T(512)S(6)} %compare.4, bf16[128,16,384]{2,1,0:T(8,128)(2,1)S(1)} %get-tuple-element.371, s32[]{:T(128)S(6)} %select_n.32, ...), kind=kOutput, calls=%fused_computation.1.clone.1 | convolution fusion | flops 146800640 | bytes 35258376 | tf_op jit(solution)/shard_map/while/body/eval_jaxpr/gct,gcr->gtr/dot_general | solution.py:70
  91.4 0.5 copy-done
  91.9 2.6 %bitcast_dynamic-update-slice_fusion.2 = f32[2,128,16,256]{3,2,1,0:T(8,128)} fusion(f32[2,128,16,256]{3,2,1,0:T(8,128)} %get-tuple-element.352, s32[]{:T(128)} %get-tuple-element.349, bf16[128,128,256]{2,1,0:T(8,128)(2,1)S(1)} %copy-done, bf16[128,256]{1,0:T(8,128)(2,1)S(1)} %get-tuple-element.332, bf16[128,16,256]{2,1,0:T(8,128)(2,1)S(1)} %get-tuple-element.370, ...), kind=kOutput, calls=%fused_computation.8.clone.1 | convolution fusion | flops 138412032 | bytes 11076100 | tf_op jit(solution)/shard_map/while/body/eval_jaxpr/gtr,gct->gcr/dot_general | solution.py:67
  94.6 3.3 %fusion.61 = f32[2,128,16,128]{3,2,1,0:T(8,128)} fusion(f32[2,128,16,128]{3,2,1,0:T(8,128)} %get-tuple-element.351, s32[]{:T(128)} %get-tuple-element.349, bf16[128,128,256]{2,1,0:T(8,128)(2,1)S(1)} %copy-done, bf16[128,256]{1,0:T(8,128)(2,1)S(1)} %get-tuple-element.332, bf16[128,16,384]{2,1,0:T(8,128)(2,1)S(1)} %get-tuple-element.371, s32[]{:T(128)S(6)} %select_n.32), kind=kOutput, calls=%fused_computation.10.clone.1 | convolution fusion | flops 138412032 | bytes 10551812 | tf_op jit(solution)/shard_map/while/body/eval_jaxpr/gtr,gcr->gct/dot_general | solution.py:64
  97.9 17.8 %copy.77 = f32[128,128,256]{0,2,1:T(8,128)} copy(f32[128,128,256]{2,1,0:T(8,128)} %get-tuple-element.146) | data formatting | bytes 33554432 | tf_op jit(solution)/shard_map/reshape | solution.py:78
  115.7 13.3 %pad.4 = f32[128,32896]{0,1:T(8,128)} pad(f32[128,32768]{0,1:T(8,128)} %bitcast.53, f32[]{:T(128)} %constant.68.clone.1), padding=0_0x0_128 | pad | bytes 33619972 | tf_op jit(solution)/shard_map/jit(_pad)/pad | solution.py:79
  129.0 17.5 %reshape.192 = f32[128,128,257]{0,2,1:T(8,128)} reshape(f32[128,32896]{0,1:T(8,128)} %pad.4) | data formatting | bytes 33685504 | tf_op jit(solution)/shard_map/reshape | solution.py:80
  146.5 6.7 %reduce_sum.27 = f32[128,257]{0,1:T(8,128)S(1)} reduce(f32[128,128,257]{0,2,1:T(8,128)} %reshape.192, f32[]{:T(128)} %constant.68.clone.1), dimensions={1}, to_apply=%region_5.6 | reduce | flops 4177792 | bytes 16974340 | tf_op jit(solution)/shard_map/reduce_sum | solution.py:81
  153.2 0.6 rev.7
  153.9 0.1 slice.31
  154.0 6.2 %collective-permute-start.1 = (bf16[128,16,128]{2,1,0:T(8,128)(2,1)S(1)}, bf16[128,16,128]{2,1,0:T(8,128)(2,1)S(1)}, u32[]{:S(2)}, u32[]{:S(2)}) collective-permute-start(bf16[128,16,128]{2,1,0:T(8,128)(2,1)S(1)} %slice.31), channel_id=1, source_target_pairs={{4,0},{8,4},{12,8},{16,12},{20,16},{24,20},{28,24},{32,28},{36,32}... | collective-permute-start | bytes 1572872 | tf_op jit(solution)/shard_map/ppermute | solution.py:15
  160.3 0.1 select_reduce_fusion.1
  160.3 0.1 fusion.43
  160.5 1.3 slice.24
  161.8 9.8 %collective-permute-done.1 = bf16[128,16,128]{2,1,0:T(8,128)(2,1)S(1)} collective-permute-done((bf16[128,16,128]{2,1,0:T(8,128)(2,1)S(1)}, bf16[128,16,128]{2,1,0:T(8,128)(2,1)S(1)}, u32[]{:S(2)}, u32[]{:S(2)}) %collective-permute-start.1) | collective-permute-done | bytes 524320 | tf_op jit(solution)/shard_map/ppermute | solution.py:15
  171.5 3.4 %fusion.38 = f32[1,128,16,128]{3,2,1,0:T(8,128)S(1)} fusion(bf16[128,16,128]{2,1,0:T(8,128)(2,1)S(1)} %collective-permute-done.1, bf16[128,128,256]{2,1,0:T(8,128)(2,1)} %get-tuple-element.382, bf16[128,128]{1,0:T(8,128)(2,1)S(1)} %slice.33), kind=kOutput, calls=%fused_computation.47 | convolution fusion | flops 69206016 | bytes 5799936 | tf_op jit(solution)/shard_map/gtr,gct->gcr/dot_general | solution.py:85
  174.9 1.9 fusion.37
  176.9 3.0 %copy.70 = f32[2,128,128,16]{1,0,3,2:T(2,128)} copy(f32[2,128,128,16]{1,3,2,0:T(8,128)S(1)} %fusion.37) | data formatting | bytes 4194304 | tf_op jit(solution)/shard_map/transpose | solution.py:90
  179.9 3.9 %reshape.190 = f32[1,256,2048]{1,2,0:T(8,128)} reshape(f32[2,128,128,16]{1,0,3,2:T(2,128)} %copy.70) | data formatting | bytes 4194304 | tf_op jit(solution)/shard_map/reshape | solution.py:90
  183.8 2.9 %fusion.33 = (bf16[1,256,2048]{1,2,0:T(8,128)(2,1)S(1)}, bf16[1,256,2048]{1,2,0:T(8,128)(2,1)}) fusion(f32[1,256,2048]{1,2,0:T(8,128)} %reshape.190, bf16[1,256,2048]{1,2,0:T(8,128)(2,1)S(1)} %copy-done.5, bf16[1,256,2048]{1,2,0:T(8,128)(2,1)S(1)} %copy-done.7), kind=kLoop, calls=%fused_computation.40 | loop fusion | flops 3145728 | bytes 6291456 | tf_op jit(solution)/shard_map/convert_element_type | solution.py:95
  186.8 2.3 copy.74
  189.0 1.4 copy.75
  190.5 4.7 %copy.68 = f32[2,128,128,16]{1,0,3,2:T(2,128)} copy(f32[2,128,128,16]{1,3,2,0:T(8,128)} %bitcast.7) | data formatting | bytes 4194304 | tf_op jit(solution)/shard_map/transpose | solution.py:91
  195.2 3.9 %reshape.188 = f32[1,256,2048]{1,2,0:T(8,128)} reshape(f32[2,128,128,16]{1,0,3,2:T(2,128)} %copy.68) | data formatting | bytes 4194304 | tf_op jit(solution)/shard_map/reshape | solution.py:91
  199.1 2.9 %fusion.32 = (bf16[1,256,2048]{1,2,0:T(8,128)(2,1)S(1)}, bf16[1,256,2048]{1,2,0:T(8,128)(2,1)}) fusion(f32[1,256,2048]{1,2,0:T(8,128)} %reshape.188, bf16[1,256,2048]{1,2,0:T(8,128)(2,1)S(1)} %copy-done.3, bf16[1,256,2048]{1,2,0:T(8,128)(2,1)S(1)} %copy-done.2), kind=kLoop, calls=%fused_computation.39 | loop fusion | flops 3145728 | bytes 6291456 | tf_op jit(solution)/shard_map/convert_element_type | solution.py:93
  202.0 2.3 copy.72
  204.2 28.5 %all-gather.3.cloned.1.call-done = f32[8192,128]{0,1:T(8,128)} async-done(((f32[128,128]{0,1:T(8,128)}), f32[8192,128]{0,1:T(8,128)}) %all-gather.3.cloned.1.call-update) | async-done | bytes 4194320 | tf_op jit(solution)/shard_map/all_gather | solution.py:97
  232.8 2.9 %copy.78 = f32[16,8,64,128]{3,2,1,0:T(8,128)S(1)} copy(f32[16,8,64,128]{3,1,2,0:T(8,128)} %bitcast.58) | data formatting | bytes 8388608
  235.7 0.6 bitcast_reduce_fusion
  236.3 0.6 multiply_reduce_fusion
  236.9 1.4 copy.73
  238.3 11.0 %psum.7 = f32[]{:T(128)} all-reduce(f32[]{:T(128)} %multiply_reduce_fusion), channel_id=1, replica_groups=mesh['dp'=2,'ctx'=32,'tensor'=4] {'tensor'}, use_global_device_ids=true, to_apply=%region_8.9 | all-reduce | flops 1 | bytes 8 | tf_op jit(solution)/shard_map/psum | solution.py:98
  250.0 0.7 copy.76
  (44 shorter events, 0.2 us)
Async XLA Ops:
  7.2 9.6 %copy-start.9 = (bf16[1,256,2048]{2,1,0:T(8,128)(2,1)S(1)}, bf16[1,256,2048]{2,1,0:T(8,128)(2,1)}, u32[]{:S(2)}) copy-start(bf16[1,256,2048]{2,1,0:T(8,128)(2,1)} %param.8) | copy-start | bytes 3145732
  7.2 225.6 %all-gather.3.cloned.1.call-start = ((), (), s32[]{:S(2)}) async-start(), calls=%async_computation | async-start | bytes 4259840 | tf_op jit(solution)/shard_map/all_gather | solution.py:97
  8.8 7.9 %copy-start.4 = (bf16[1,256,2048]{1,2,0:T(8,128)(2,1)}, bf16[1,256,2048]{1,2,0:T(8,128)(2,1)S(1)}, u32[]{:S(2)}) copy-start(bf16[1,256,2048]{1,2,0:T(8,128)(2,1)S(1)} %copy.63) | copy-start | bytes 3145732
  10.7 9.3 %copy-start.6 = (bf16[1,256,2048]{1,2,0:T(8,128)(2,1)}, bf16[1,256,2048]{1,2,0:T(8,128)(2,1)S(1)}, u32[]{:S(2)}) copy-start(bf16[1,256,2048]{1,2,0:T(8,128)(2,1)S(1)} %copy.64) | copy-start | bytes 3145732
  10.7 9.2 %copy-start.10 = (bf16[128,128]{1,0:T(8,128)(2,1)S(1)}, bf16[128,128]{1,0:T(8,128)(2,1)}, u32[]{:S(2)}) copy-start(bf16[128,128]{1,0:T(8,128)(2,1)} %param.13) | copy-start | bytes 98308
  11.0 1.0 copy-start.8
  12.9 45.9 %collective-permute-start = (bf16[128,16,128]{2,1,0:T(8,128)(2,1)}, bf16[128,16,128]{2,1,0:T(8,128)(2,1)}, u32[]{:S(2)}, u32[]{:S(2)}) collective-permute-start(bf16[128,16,128]{2,1,0:T(8,128)(2,1)} %slice.29), channel_id=1, source_target_pairs={{0,4},{4,8},{8,12},{12,16},{16,20},{20,24},{24,28},{28,32},{32,36}... | collective-permute-start | bytes 1572872 | tf_op jit(solution)/shard_map/ppermute | solution.py:15
  17.3 40.0 %copy-start.1 = (bf16[1,256,2048]{1,2,0:T(8,128)(2,1)}, bf16[1,256,2048]{1,2,0:T(8,128)(2,1)S(1)}, u32[]{:S(2)}) copy-start(bf16[1,256,2048]{1,2,0:T(8,128)(2,1)S(1)} %copy.61) | copy-start | bytes 3145732
  44.8 12.2 %copy-start.11 = (s32[1,64]{1,0:T(1,128)S(1)}, s32[1,64]{1,0:T(1,128)}, u32[]{:S(2)}) copy-start(s32[1,64]{1,0:T(1,128)} %param.12) | copy-start | bytes 772
  62.5 7.9 %copy-start = (bf16[128,128,256]{2,1,0:T(8,128)(2,1)S(1)}, bf16[128,128,256]{2,1,0:T(8,128)(2,1)}, u32[]{:S(2)}) copy-start(bf16[128,128,256]{2,1,0:T(8,128)(2,1)} %get-tuple-element.374) | copy-start | bytes 25165828 | tf_op jit(solution)/shard_map/while
  78.5 13.5 %copy-start = (bf16[128,128,256]{2,1,0:T(8,128)(2,1)S(1)}, bf16[128,128,256]{2,1,0:T(8,128)(2,1)}, u32[]{:S(2)}) copy-start(bf16[128,128,256]{2,1,0:T(8,128)(2,1)} %get-tuple-element.374) | copy-start | bytes 25165828 | tf_op jit(solution)/shard_map/while
  154.0 17.6 %collective-permute-start.1 = (bf16[128,16,128]{2,1,0:T(8,128)(2,1)S(1)}, bf16[128,16,128]{2,1,0:T(8,128)(2,1)S(1)}, u32[]{:S(2)}, u32[]{:S(2)}) collective-permute-start(bf16[128,16,128]{2,1,0:T(8,128)(2,1)S(1)} %slice.31), channel_id=1, source_target_pairs={{4,0},{8,4},{12,8},{16,12},{20,16},{24,20},{28,24},{32,28},{36,32}... | collective-permute-start | bytes 1572872 | tf_op jit(solution)/shard_map/ppermute | solution.py:15
  176.9 6.9 %copy-start.5 = (bf16[1,256,2048]{1,2,0:T(8,128)(2,1)S(1)}, bf16[1,256,2048]{1,2,0:T(8,128)(2,1)}, u32[]{:S(2)}) copy-start(bf16[1,256,2048]{1,2,0:T(8,128)(2,1)} %copy-done.4) | copy-start | bytes 3145732
  176.9 6.9 %copy-start.7 = (bf16[1,256,2048]{1,2,0:T(8,128)(2,1)S(1)}, bf16[1,256,2048]{1,2,0:T(8,128)(2,1)}, u32[]{:S(2)}) copy-start(bf16[1,256,2048]{1,2,0:T(8,128)(2,1)} %copy-done.6) | copy-start | bytes 3145732
  190.4 8.6 %copy-start.2 = (bf16[1,256,2048]{1,2,0:T(8,128)(2,1)S(1)}, bf16[1,256,2048]{1,2,0:T(8,128)(2,1)}, u32[]{:S(2)}) copy-start(bf16[1,256,2048]{1,2,0:T(8,128)(2,1)} %copy-done.1) | copy-start | bytes 3145732
  190.4 8.6 %copy-start.3 = (bf16[1,256,2048]{1,2,0:T(8,128)(2,1)S(1)}, bf16[1,256,2048]{1,2,0:T(8,128)(2,1)}, u32[]{:S(2)}) copy-start(bf16[1,256,2048]{1,2,0:T(8,128)(2,1)} %copy.62) | copy-start | bytes 3145732
Sparse Core Ops, SparseCore 0:
  154.0 78.7 all-gather.2
